TPU v7x, 128 devices: a whole 4x4x4 slice. The times are simulated.
128 devices in a mesh: seq: 64 (over z, x, y_lo, core), chan: 2 (over y_hi).
Axes of the slice: x: 4, y: 4 (y_hi: 2, y_lo: 2; y = y_hi * 2 + y_lo), z: 4, core: 2. Of those that a mesh axis runs over, the one named last changes fastest.
Arguments:
- signal: bfloat16 [2, 32768, 128], P('chan', 'seq'), may hold values from -6 to 6
- cotangent: bfloat16 [2, 32768, 128], P('chan', 'seq'), may hold values from -6 to 6
- band_freq: int32 [16], replicated, may hold values from 1 to 8191
- w_embed: float32 [32, 64], replicated, may hold values from -2 to 2
- b_embed: float32 [64], replicated, may hold values from -3.140625 to 3.140625
- w_out: float32 [64, 128], P(None, 'chan'), may hold values from -0.75 to 0.75
- decay: float32 [128], P('chan'), may hold values from 0.25 to 16, as said below
Outputs:
- conv_out: bfloat16 [2, 32768, 128], P('chan', 'seq')
- d_signal: bfloat16 [2, 32768, 128], P('chan', 'seq')
- grad_embed: float32 [32, 64], replicated
- grad_bias: float32 [64], replicated
- grad_out: float32 [64, 128], P(None, 'chan')
Inputs may be any that keep to these rules, and one draw needn't show every extreme that they name: decay rates are positive.
All inputs are finite; a program needn't handle non-finite values.
Results may differ from a plain program's by a relative error of at most 0.007.
Values may be sent and summed in bfloat16 or wider, within the bound.
No kernel may reach another device: no remote copies, remote signals or barrier semaphores. Data moves between devices by JAX's collectives and lax.ppermute only.
A program may use at most 192 MiB of HBM per device.

v0:
```python
import math
import jax
import jax.numpy as jnp
from jax import lax
from jax.sharding import PartitionSpec as P

exact_mode = lax.Precision.HIGHEST


def mat_dot(lhs_mat, rhs_mat):
    return jnp.dot(lhs_mat, rhs_mat, preferred_element_type=jnp.float32, precision=exact_mode)


def band_phase(band_freq, places, seq_total):
    upper_part = places // 1024
    lower_part = places % 1024
    partial_turn = upper_part[:, None] * band_freq[None, :] % seq_total
    wrapped = (partial_turn * 1024 + lower_part[:, None] * band_freq[None, :]) % seq_total
    return wrapped.astype(jnp.float32) * (2.0 * math.pi / seq_total)


def filter_parts(places, band_freq, w_embed, b_embed, w_out, decay, seq_total):
    phases = band_phase(band_freq, places, seq_total)
    features = jnp.concatenate([jnp.cos(phases), jnp.sin(phases)], axis=1)
    preact = mat_dot(features, w_embed) + b_embed[None, :]
    hidden = jnp.sin(preact)
    fraction = places.astype(jnp.float32) / seq_total
    envelope = (
        jnp.exp(-decay[None, :] * fraction[:, None]) * jnp.sqrt((1.0 + decay) / seq_total)[None, :]
    )
    taps = mat_dot(hidden, w_out) * envelope
    return (features, preact, hidden, taps, envelope)


def angle_table(rows_idx, cols_idx, modulus):
    wrapped = rows_idx[:, None] * cols_idx[None, :] % modulus
    angles = wrapped.astype(jnp.float32) * (2.0 * math.pi / modulus)
    return (jnp.cos(angles), jnp.sin(angles))


def local(signal, cotangent, band_freq, w_embed, b_embed, w_out, decay):
    devices = lax.axis_size("seq")
    rank_seq = lax.axis_index("seq")
    seg_len = signal.shape[1] * 2
    channels = signal.shape[2] // 2
    block_w = seg_len // devices
    width = block_w * channels
    rows_all = 2 * devices
    pair = rows_all // devices
    seq_total = seg_len * devices
    fft_size = 2 * seq_total
    inv_scale = 1.0 / fft_size
    n_arr = 3
    dev_ids = jnp.arange(devices, dtype=jnp.int32)
    row_ids = jnp.arange(rows_all, dtype=jnp.int32)
    blk_ids = jnp.arange(block_w, dtype=jnp.int32)
    lane_blk = jnp.arange(width, dtype=jnp.int32) // channels
    b_lane = rank_seq * block_w + lane_blk
    src = jnp.stack([signal.reshape(devices, width), cotangent.reshape(devices, width)], axis=1)
    cols = lax.all_to_all(src, "seq", split_axis=0, concat_axis=0, tiled=True)
    places = (dev_ids[:, None] * seg_len + rank_seq * block_w + blk_ids[None, :]).reshape(-1)
    features, preact, hidden, taps, envelope = filter_parts(
        places, band_freq, w_embed, b_embed, w_out, decay, seq_total
    )
    stacked = jnp.concatenate(
        [cols.astype(jnp.float32), taps.reshape(devices, 1, width)], axis=1
    ).reshape(devices, n_arr * width)
    col_cos, col_sin = angle_table(row_ids, dev_ids, rows_all)
    y_re = mat_dot(col_cos, stacked).reshape(rows_all, n_arr, width)
    y_im = -mat_dot(col_sin, stacked).reshape(rows_all, n_arr, width)
    tw_cos, tw_sin = angle_table(row_ids, b_lane, fft_size)
    tw_cos = tw_cos[:, None, :]
    tw_sin = tw_sin[:, None, :]
    t_re = y_re * tw_cos + y_im * tw_sin
    t_im = y_im * tw_cos - y_re * tw_sin
    spec = jnp.stack([t_re, t_im], axis=1)
    spec = lax.all_to_all(spec, "seq", split_axis=0, concat_axis=0, tiled=True)
    q_cos, q_sin = angle_table(dev_ids, dev_ids, devices)
    stage_a = mat_dot(jnp.concatenate([q_cos, q_sin], axis=0), spec.reshape(devices, -1))
    stage_a = stage_a.reshape(2, devices, pair, 2, n_arr, width)
    a_re = stage_a[0, :, :, 0] + stage_a[1, :, :, 1]
    a_im = stage_a[0, :, :, 1] - stage_a[1, :, :, 0]
    mid_cos, mid_sin = angle_table(dev_ids, lane_blk, seg_len)
    mid_cos = mid_cos[:, None, None, :]
    mid_sin = mid_sin[:, None, None, :]
    b_re = (a_re * mid_cos + a_im * mid_sin).reshape(devices, pair, n_arr, block_w, channels)
    b_im = (a_im * mid_cos - a_re * mid_sin).reshape(devices, pair, n_arr, block_w, channels)
    m_cos, m_sin = angle_table(blk_ids, blk_ids, block_w)

    def blk_mix(table, vals):
        return jnp.einsum(
            "mb,qkzbc->qkzmc", table, vals, preferred_element_type=jnp.float32, precision=exact_mode
        )

    s_re = blk_mix(m_cos, b_re) + blk_mix(m_sin, b_im)
    s_im = blk_mix(m_cos, b_im) - blk_mix(m_sin, b_re)
    sig_r, cot_r, tap_r = (s_re[:, :, 0], s_re[:, :, 1], s_re[:, :, 2])
    sig_i, cot_i, tap_i = (s_im[:, :, 0], s_im[:, :, 1], s_im[:, :, 2])
    prod_r = jnp.stack(
        [
            sig_r * tap_r - sig_i * tap_i,
            cot_r * tap_r + cot_i * tap_i,
            cot_r * sig_r + cot_i * sig_i,
        ],
        axis=2,
    )
    prod_i = jnp.stack(
        [
            sig_r * tap_i + sig_i * tap_r,
            cot_i * tap_r - cot_r * tap_i,
            cot_i * sig_r - cot_r * sig_i,
        ],
        axis=2,
    )
    u_re = blk_mix(m_cos, prod_r) - blk_mix(m_sin, prod_i)
    u_im = blk_mix(m_cos, prod_i) + blk_mix(m_sin, prod_r)
    u_re = u_re.reshape(devices, pair, n_arr, width)
    u_im = u_im.reshape(devices, pair, n_arr, width)
    v_re = u_re * mid_cos - u_im * mid_sin
    v_im = u_im * mid_cos + u_re * mid_sin
    v_all = jnp.stack([v_re, v_im]).reshape(2 * devices, -1)
    inv_mat = jnp.concatenate(
        [jnp.concatenate([q_cos, -q_sin], axis=1), jnp.concatenate([q_sin, q_cos], axis=1)], axis=0
    )
    w_all = mat_dot(inv_mat, v_all).reshape(2, devices, pair, n_arr, width)
    b_rows = dev_ids[:, None] * block_w + lane_blk[None, :]
    k1_own = rank_seq * pair + jnp.arange(pair, dtype=jnp.int32)
    ex_ang = b_rows[:, None, :] * k1_own[None, :, None] % fft_size
    ex_ang = ex_ang.astype(jnp.float32) * (2.0 * math.pi / fft_size)
    ex_cos = jnp.cos(ex_ang)[:, :, None, :]
    ex_sin = jnp.sin(ex_ang)[:, :, None, :]
    x_re = w_all[0] * ex_cos - w_all[1] * ex_sin
    x_im = w_all[0] * ex_sin + w_all[1] * ex_cos
    back = jnp.stack([x_re, x_im], axis=1)
    back = lax.all_to_all(back, "seq", split_axis=0, concat_axis=0, tiled=True)
    back = back.reshape(devices, 2, pair, n_arr * width)
    back = jnp.transpose(back, (1, 0, 2, 3)).reshape(2 * rows_all, n_arr * width)
    out_mat = jnp.concatenate([col_cos.T, -col_sin.T], axis=1)
    res = (mat_dot(out_mat, back) * inv_scale).reshape(devices, n_arr, width)
    rows_out = lax.all_to_all(
        res[:, 0:2].astype(jnp.bfloat16), "seq", split_axis=0, concat_axis=0, tiled=True
    )
    conv_out = rows_out[:, 0].reshape(1, seg_len // 2, 2 * channels)
    d_signal = rows_out[:, 1].reshape(1, seg_len // 2, 2 * channels)
    d_taps = res[:, 2].reshape(devices * block_w, channels)
    d_raw = d_taps * envelope
    d_preact = mat_dot(d_raw, w_out.T) * jnp.cos(preact)
    out_part = mat_dot(hidden.T, d_raw)
    embed_part = mat_dot(features.T, d_preact)
    bias_part = jnp.sum(d_preact, axis=0)
    out_sum = lax.psum(out_part, "seq")
    embed_all, bias_all = lax.psum((embed_part, bias_part), ("seq", "chan"))
    norm_scale = 1.0 / math.sqrt(seq_total)
    return (conv_out, d_signal, embed_all * norm_scale, bias_all * norm_scale, out_sum * norm_scale)


def solution(mesh):
    return jax.shard_map(
        local,
        mesh=mesh,
        in_specs=(
            P("chan", "seq", None),
            P("chan", "seq", None),
            P(),
            P(),
            P(),
            P(None, "chan"),
            P("chan"),
        ),
        out_specs=(P("chan", "seq", None), P("chan", "seq", None), P(), P(), P(None, "chan")),
        check_vma=False,
    )
```

profile of v0, /device:TPU:0, one launch (start us, length us, event | category | flops | bytes accessed | tf_op | source)
XLA Modules:
  0.0 615.8 jit_solution(7838954913175535610)
XLA Ops:
  0.6 1.2 stack_reshape.8
  1.9 1.2 stack_reshape.9
  3.1 1.3 pad_maximum_fusion.14
  4.4 9.9 %all-to-all-start = ((bf16[64,2,1024]{2,1,0:T(2,128)(2,1)}), bf16[64,2,1024]{2,1,0:T(2,128)(2,1)S(1)}, u32[]{:S(2)}, u32[]{:S(2)}) async-start(bf16[64,2,1024]{2,1,0:T(2,128)(2,1)} %pad_maximum_fusion.14), calls=%async_computation | async-start | bytes 524288 | tf_op jit(solution)/shard_map/all_to_all | solution.py:60
  14.5 0.7 fusion.180
  15.2 1.0 fusion.84
  16.2 2.7 fusion.181
  19.9 2.0 fusion.35
  21.9 2.3 all-to-all-done
  24.9 1.9 convolution_negate_fusion
  26.8 2.3 add_bitcast_fusion.2
  29.3 4.1 copy.76
  33.4 6.9 %all-to-all-start.1 = ((f32[128,2,3,1024]{3,1,2,0:T(2,128)}), f32[128,2,3,1024]{3,1,2,0:T(2,128)S(1)}, u32[]{:S(2)}, u32[]{:S(2)}) async-start(f32[128,2,3,1024]{3,1,2,0:T(2,128)} %copy.76), calls=%async_computation.1 | async-start | bytes 6291456 | tf_op jit(solution)/shard_map/all_to_all | solution.py:77
  40.3 0.8 fusion.100
  42.6 1.8 fusion.44
  44.4 2.9 fusion.33
  47.2 9.5 %fusion.38 = (f32[64,2,1024]{2,1,0:T(2,128)}, f32[64,2,1024]{2,1,0:T(2,128)}) fusion(s32[2]{0:T(128)S(1)} %iota_add_fusion.1, s32[64,1024]{1,0:T(8,128)S(1)} %broadcast_add_fusion), kind=kLoop, calls=%fused_computation.88 | loop fusion | flops 1835008 | bytes 1310728 | tf_op jit(solution)/shard_map/cos | solution.py:130
  56.8 23.2 %all-to-all-done.1 = f32[128,2,3,1024]{3,1,2,0:T(2,128)S(1)} async-done(((f32[128,2,3,1024]{3,1,2,0:T(2,128)}), f32[128,2,3,1024]{3,1,2,0:T(2,128)S(1)}, u32[]{:S(2)}, u32[]{:S(2)}) %all-to-all-start.1) | async-done | bytes 3145760 | tf_op jit(solution)/shard_map/all_to_all | solution.py:77
  80.0 3.7 copy.77
  83.7 4.3 reshape.397
  88.0 3.7 dot_general.72
  91.8 9.4 %fusion = f32[2,64,2,2,3,1024]{5,1,4,3,2,0:T(8,128)S(1)} fusion(f32[2,64,64,1,1,1]{2,1,5,4,3,0:T(8,128)} %bitcast.98, f32[2,2,3,1024,64]{3,2,1,0,4:T(4,128)} %dot_general.72), kind=kOutput, calls=%fused_computation.6 | convolution fusion | flops 1207959552 | bytes 9469952 | tf_op jit(solution)/shard_map/dot_general | solution.py:11
  101.2 2.7 slice_add_fusion
  103.8 2.5 add.319
  106.4 3.6 sub.92
  110.0 5.5 fusion.51
  115.5 3.3 fusion.52
  118.8 3.3 add_bitcast_fusion.1
  122.1 3.5 subtract_bitcast_fusion.1
  126.2 0.7 multiply_subtract_fusion.5
  126.9 3.0 fusion.4
  130.0 2.9 fusion.3
  132.9 4.7 subtract_bitcast_fusion
  137.6 4.9 reshape.411
  142.5 6.4 %add_bitcast_fusion = f32[64,2,3,16,64]{4,3,2,1,0:T(8,128)} fusion(f32[64,2,3,64,16]{3,4,2,1,0:T(8,128)S(1)} %fusion.3, f32[64,2,1,16,64]{4,3,2,1,0:T(8,128)} %copy-done.5, f32[64,2,1,16,64]{4,3,2,1,0:T(8,128)} %copy-done.6, f32[64,2,1,16,64]{4,3,2,1,0:T(8,128)} %copy-done.4), kind=kOutput, calls=%fused_computation.9 | convolution fusion | flops 76680704 | bytes 4718592 | tf_op jit(solution)/shard_map/mb,qkzbc->qkzmc/dot_general | solution.py:91
  148.9 4.6 reshape.412
  153.6 3.3 multiply_subtract_fusion.2
  157.1 4.1 copy.85
  161.2 5.0 reshape.400
  166.2 3.8 fusion.63
  170.0 1.8 fusion.179
  171.9 3.1 squeeze.4
  174.9 3.9 squeeze.5
  178.9 2.4 multiply_subtract_fusion.1
  181.3 1.6 pad_maximum_fusion
  182.9 4.7 copy.86
  187.5 6.6 %all-to-all-start.2 = ((f32[64,2,2,3,1024]{4,2,3,1,0:T(2,128)}), f32[64,2,2,3,1024]{4,2,3,1,0:T(2,128)S(1)}, u32[]{:S(2)}, u32[]{:S(2)}) async-start(f32[64,2,2,3,1024]{4,2,3,1,0:T(2,128)} %copy.86), calls=%async_computation.2 | async-start | bytes 6291456 | tf_op jit(solution)/shard_map/all_to_all | solution.py:135
  194.1 0.8 sine_negate_fusion
  194.9 38.9 %all-to-all-done.2 = f32[64,2,2,3,1024]{4,2,3,1,0:T(2,128)S(1)} async-done(((f32[64,2,2,3,1024]{4,2,3,1,0:T(2,128)}), f32[64,2,2,3,1024]{4,2,3,1,0:T(2,128)S(1)}, u32[]{:S(2)}, u32[]{:S(2)}) %all-to-all-start.2) | async-done | bytes 3145760 | tf_op jit(solution)/shard_map/all_to_all | solution.py:135
  233.8 3.6 copy.87
  237.4 5.0 reshape.401
  242.3 4.1 copy.88
  246.4 3.9 reshape.402
  250.3 3.7 convolution_multiply_fusion
  254.0 1.7 reshape.403
  255.7 0.7 slice_reduce_fusion
  256.5 0.9 slice.117
  258.2 1.3 fusion.182
  259.9 64.6 %all-reduce = (f32[32,64]{1,0:T(8,128)S(1)}, f32[64]{0:T(128)S(1)}) all-reduce(f32[32,64]{1,0:T(8,128)S(1)} %fusion.53, f32[64]{0:T(128)S(1)} %get-tuple-element.41), channel_id=1, replica_groups=mesh['seq'=64,'chan'=2] {'seq','chan'}, use_global_device_ids=true, to_apply=%region_0.1 | all-reduce | flops 2112 | bytes 16896 | tf_op jit(solution)/shard_map/psum | solution.py:152
  325.1 5.9 all-to-all-start.3
  331.5 280.7 %psum.23 = f32[64,64]{1,0:T(8,128)S(1)} all-reduce(f32[64,64]{1,0:T(8,128)S(1)} %fusion.40), channel_id=1, replica_groups=mesh['seq'=64,'chan'=2] {'seq'}, use_global_device_ids=true, to_apply=%region_3.4 | all-reduce | flops 4096 | bytes 32768 | tf_op jit(solution)/shard_map/psum | solution.py:151
  612.8 1.1 slice_reduce_fusion.1
  613.9 0.7 reshape_squeeze.10
  614.6 0.7 reshape_squeeze.9
  (61 shorter events, 7.2 us)
Async XLA Ops:
  0.6 18.3 %copy-start = (f32[64,64]{1,0:T(8,128)S(1)}, f32[64,64]{1,0:T(8,128)}, u32[]{:S(2)}) copy-start(f32[64,64]{1,0:T(8,128)} %param.12) | copy-start | bytes 49156
  4.4 19.8 %all-to-all-start = ((bf16[64,2,1024]{2,1,0:T(2,128)(2,1)}), bf16[64,2,1024]{2,1,0:T(2,128)(2,1)S(1)}, u32[]{:S(2)}, u32[]{:S(2)}) async-start(bf16[64,2,1024]{2,1,0:T(2,128)(2,1)} %pad_maximum_fusion.14), calls=%async_computation | async-start | bytes 524288 | tf_op jit(solution)/shard_map/all_to_all | solution.py:60
  16.2 2.7 copy-start.13
  33.4 46.6 %all-to-all-start.1 = ((f32[128,2,3,1024]{3,1,2,0:T(2,128)}), f32[128,2,3,1024]{3,1,2,0:T(2,128)S(1)}, u32[]{:S(2)}, u32[]{:S(2)}) async-start(f32[128,2,3,1024]{3,1,2,0:T(2,128)} %copy.76), calls=%async_computation.1 | async-start | bytes 6291456 | tf_op jit(solution)/shard_map/all_to_all | solution.py:77
  41.2 0.6 copy-start.15
  109.9 5.5 copy-start.1
  110.0 5.5 copy-start.2
  110.0 5.5 copy-start.3
  126.2 6.8 %copy-start.6 = (f32[64,2,1,16,64]{4,3,2,1,0:T(8,128)}, f32[64,2,1,16,64]{4,3,2,1,0:T(8,128)S(1)}, u32[]{:S(2)}) copy-start(f32[64,2,1,16,64]{4,3,2,1,0:T(8,128)S(1)} %get-tuple-element.13) | copy-start | bytes 1572868
  126.9 6.0 copy-start.4
  126.9 6.0 copy-start.5
  148.9 4.6 copy-start.7
  148.9 4.6 copy-start.10
  148.9 4.6 copy-start.11
  171.9 7.0 %copy-start.8 = (f32[64,2,1024]{2,1,0:T(2,128)S(1)}, f32[64,2,1024]{2,1,0:T(2,128)}, u32[]{:S(2)}) copy-start(f32[64,2,1024]{2,1,0:T(2,128)} %get-tuple-element.25) | copy-start | bytes 1572868
  171.9 7.0 %copy-start.9 = (f32[64,2,1024]{2,1,0:T(2,128)S(1)}, f32[64,2,1024]{2,1,0:T(2,128)}, u32[]{:S(2)}) copy-start(f32[64,2,1024]{2,1,0:T(2,128)} %get-tuple-element.26) | copy-start | bytes 1572868
  187.5 46.3 %all-to-all-start.2 = ((f32[64,2,2,3,1024]{4,2,3,1,0:T(2,128)}), f32[64,2,2,3,1024]{4,2,3,1,0:T(2,128)S(1)}, u32[]{:S(2)}, u32[]{:S(2)}) async-start(f32[64,2,2,3,1024]{4,2,3,1,0:T(2,128)} %copy.86), calls=%async_computation.2 | async-start | bytes 6291456 | tf_op jit(solution)/shard_map/all_to_all | solution.py:135
  254.0 4.2 copy-start.12
  254.0 5.6 copy-start.14
  325.1 287.8 %all-to-all-start.3 = ((bf16[64,2,1024]{2,1,0:T(2,128)(2,1)}), bf16[64,2,1024]{2,1,0:T(2,128)(2,1)S(1)}, u32[]{:S(2)}, u32[]{:S(2)}) async-start(bf16[64,2,1024]{2,1,0:T(2,128)(2,1)} %slice.117), calls=%async_computation.3 | async-start | bytes 524288 | tf_op jit(solution)/shard_map/all_to_all | solution.py:140
where the time goes:
time: 627 us; the launch traced here: 616 us
  blocking collectives  345 us (55%)
  local copies, waits for them, and re-layouts  80.4 us (13%)
  waiting for transfers between devices  64.5 us (10%)
  matrix products  58.9 us (9%)
  other arithmetic  35.8 us (6%)
  starting transfers between devices  29.3 us (5%)
    psum x1, blocking collectives, local(): out_sum = lax.psum(out_part, 'seq')  281 us
    psum x1, blocking collectives, local(): embed_all, bias_all = lax.psum((embed_part, bias_part), ('seq', 'chan'))  64.6 us
    all_to_all x1, waiting for transfers between devices, local(): back = lax.all_to_all(back, 'seq', split_axis=0, concat_axis=0, tiled=True)  38.9 us
    dot_general x8, matrix products, blk_mix(): jnp.einsum('mb,qkzbc->qkzmc', table, vals, preferred_element_type=jnp.flo...  32.6 us
    dot_general x10, matrix products, mat_dot(): jnp.dot(lhs_mat, rhs_mat, preferred_element_type=jnp.float32, precision=e...  26.2 us
    all_to_all x1, waiting for transfers between devices, local(): spec = lax.all_to_all(spec, 'seq', split_axis=0, concat_axis=0, tiled=True)  23.2 us
  transfers between devices with their start and end apart: 4, of which 3 were waited for; matrix products, arithmetic and copies ran while one was open for 4% of the time, Pallas kernels for 0%

commit v1 on v0

--- a/solution.py
+++ b/solution.py
@@ -1,3 +1,4 @@
+import functools
 import math
 import jax
 import jax.numpy as jnp
@@ -5,6 +6,15 @@
 from jax.sharding import PartitionSpec as P
 
 exact_mode = lax.Precision.HIGHEST
+
+
+def group_the_waves(inp, shard_axis, which_axis):
+    for hop_no in (shard_axis, which_axis):
+        inp = lax.psum(inp, hop_no)
+    return inp
+
+
+_try_all_point = functools.partial(group_the_waves, shard_axis="chan", which_axis="seq")
 
 
 def mat_dot(lhs_mat, rhs_mat):
@@ -149,7 +159,7 @@
     embed_part = mat_dot(features.T, d_preact)
     bias_part = jnp.sum(d_preact, axis=0)
     out_sum = lax.psum(out_part, "seq")
-    embed_all, bias_all = lax.psum((embed_part, bias_part), ("seq", "chan"))
+    embed_all, bias_all = _try_all_point((embed_part, bias_part))
     norm_scale = 1.0 / math.sqrt(seq_total)
     return (conv_out, d_signal, embed_all * norm_scale, bias_all * norm_scale, out_sum * norm_scale)
 

time: 627 us -> 576 us (0.919)
  the two profiles are of different devices: /device:TPU:0 before, /device:TPU:1 now
where the time goes in v1:
time: 576 us; the launch traced here: 565 us
  blocking collectives  280 us (49%)
  local copies, waits for them, and re-layouts  80.5 us (14%)
  waiting for transfers between devices  73.5 us (13%)
  matrix products  58.9 us (10%)
  other arithmetic  35.8 us (6%)
  starting transfers between devices  34.9 us (6%)
    psum x2, blocking collectives, group_the_waves(): inp = lax.psum(inp, hop_no)  280 us
    all_to_all x1, waiting for transfers between devices, local(): back = lax.all_to_all(back, 'seq', split_axis=0, concat_axis=0, tiled=True)  39.3 us
    dot_general x8, matrix products, blk_mix(): jnp.einsum('mb,qkzbc->qkzmc', table, vals, preferred_element_type=jnp.flo...  32.7 us
    dot_general x10, matrix products, mat_dot(): jnp.dot(lhs_mat, rhs_mat, preferred_element_type=jnp.float32, precision=e...  26.2 us
    all_to_all x1, waiting for transfers between devices, local(): spec = lax.all_to_all(spec, 'seq', split_axis=0, concat_axis=0, tiled=True)  23.7 us
  transfers between devices with their start and end apart: 4, of which 4 were waited for; matrix products, arithmetic and copies ran while one was open for 4% of the time, Pallas kernels for 0%

profile of v1, /device:TPU:1, one launch (start us, length us, event | category | flops | bytes accessed | tf_op | source)
XLA Modules:
  0.0 565.0 jit_solution(8643069451464559887)
XLA Ops:
  0.6 1.2 stack_reshape.8
  1.9 1.2 stack_reshape.9
  3.1 1.3 pad_maximum_fusion.14
  4.4 10.8 %all-to-all-start = ((bf16[64,2,1024]{2,1,0:T(2,128)(2,1)}), bf16[64,2,1024]{2,1,0:T(2,128)(2,1)S(1)}, u32[]{:S(2)}, u32[]{:S(2)}) async-start(bf16[64,2,1024]{2,1,0:T(2,128)(2,1)} %pad_maximum_fusion.14), calls=%async_computation | async-start | bytes 524288 | tf_op jit(solution)/shard_map/all_to_all | solution.py:70
  16.1 1.0 fusion.84
  17.2 2.7 fusion.181
  20.8 2.0 fusion.35
  22.9 2.0 all-to-all-done
  25.5 1.9 convolution_negate_fusion
  27.4 2.3 add_bitcast_fusion.2
  29.9 4.1 copy.76
  34.0 7.2 %all-to-all-start.1 = ((f32[128,2,3,1024]{3,1,2,0:T(2,128)}), f32[128,2,3,1024]{3,1,2,0:T(2,128)S(1)}, u32[]{:S(2)}, u32[]{:S(2)}) async-start(f32[128,2,3,1024]{3,1,2,0:T(2,128)} %copy.76), calls=%async_computation.1 | async-start | bytes 6291456 | tf_op jit(solution)/shard_map/all_to_all | solution.py:87
  41.3 0.7 fusion.100
  43.5 1.8 fusion.44
  45.3 2.9 fusion.33
  48.2 9.5 %fusion.38 = (f32[64,2,1024]{2,1,0:T(2,128)}, f32[64,2,1024]{2,1,0:T(2,128)}) fusion(s32[2]{0:T(128)S(1)} %iota_add_fusion.1, s32[64,1024]{1,0:T(8,128)S(1)} %broadcast_add_fusion), kind=kLoop, calls=%fused_computation.88 | loop fusion | flops 1835008 | bytes 1310728 | tf_op jit(solution)/shard_map/cos | solution.py:140
  57.7 23.7 %all-to-all-done.1 = f32[128,2,3,1024]{3,1,2,0:T(2,128)S(1)} async-done(((f32[128,2,3,1024]{3,1,2,0:T(2,128)}), f32[128,2,3,1024]{3,1,2,0:T(2,128)S(1)}, u32[]{:S(2)}, u32[]{:S(2)}) %all-to-all-start.1) | async-done | bytes 3145760 | tf_op jit(solution)/shard_map/all_to_all | solution.py:87
  81.4 3.7 copy.77
  85.1 4.3 reshape.397
  89.4 3.7 dot_general.72
  93.2 9.4 %fusion = f32[2,64,2,2,3,1024]{5,1,4,3,2,0:T(8,128)S(1)} fusion(f32[2,64,64,1,1,1]{2,1,5,4,3,0:T(8,128)} %bitcast.98, f32[2,2,3,1024,64]{3,2,1,0,4:T(4,128)} %dot_general.72), kind=kOutput, calls=%fused_computation.6 | convolution fusion | flops 1207959552 | bytes 9469952 | tf_op jit(solution)/shard_map/dot_general | solution.py:21
  102.6 2.7 slice_add_fusion
  105.2 2.5 add.323
  107.7 3.6 sub.92
  111.4 5.5 fusion.51
  116.9 3.3 fusion.52
  120.2 3.3 add_bitcast_fusion.1
  123.5 3.5 subtract_bitcast_fusion.1
  127.6 0.7 multiply_subtract_fusion.5
  128.3 3.0 fusion.4
  131.4 2.9 fusion.3
  134.4 4.7 subtract_bitcast_fusion
  139.0 4.9 reshape.411
  143.9 6.4 %add_bitcast_fusion = f32[64,2,3,16,64]{4,3,2,1,0:T(8,128)} fusion(f32[64,2,3,64,16]{3,4,2,1,0:T(8,128)S(1)} %fusion.3, f32[64,2,1,16,64]{4,3,2,1,0:T(8,128)} %copy-done.5, f32[64,2,1,16,64]{4,3,2,1,0:T(8,128)} %copy-done.6, f32[64,2,1,16,64]{4,3,2,1,0:T(8,128)} %copy-done.4), kind=kOutput, calls=%fused_computation.9 | convolution fusion | flops 76680704 | bytes 4718592 | tf_op jit(solution)/shard_map/mb,qkzbc->qkzmc/dot_general | solution.py:101
  150.3 4.6 reshape.412
  155.0 3.3 multiply_subtract_fusion.2
  158.6 4.1 copy.85
  162.7 5.0 reshape.400
  167.6 3.8 fusion.63
  171.4 1.8 fusion.179
  173.3 3.1 squeeze.4
  176.4 3.9 squeeze.5
  180.3 2.4 multiply_subtract_fusion.1
  182.7 1.6 pad_maximum_fusion
  184.3 4.7 copy.86
  188.9 6.3 %all-to-all-start.2 = ((f32[64,2,2,3,1024]{4,2,3,1,0:T(2,128)}), f32[64,2,2,3,1024]{4,2,3,1,0:T(2,128)S(1)}, u32[]{:S(2)}, u32[]{:S(2)}) async-start(f32[64,2,2,3,1024]{4,2,3,1,0:T(2,128)} %copy.86), calls=%async_computation.2 | async-start | bytes 6291456 | tf_op jit(solution)/shard_map/all_to_all | solution.py:145
  195.2 0.8 sine_negate_fusion
  196.0 39.3 %all-to-all-done.2 = f32[64,2,2,3,1024]{4,2,3,1,0:T(2,128)S(1)} async-done(((f32[64,2,2,3,1024]{4,2,3,1,0:T(2,128)}), f32[64,2,2,3,1024]{4,2,3,1,0:T(2,128)S(1)}, u32[]{:S(2)}, u32[]{:S(2)}) %all-to-all-start.2) | async-done | bytes 3145760 | tf_op jit(solution)/shard_map/all_to_all | solution.py:145
  235.3 3.6 copy.87
  238.9 5.0 reshape.401
  243.8 4.1 copy.88
  247.9 3.9 reshape.402
  251.8 3.7 convolution_multiply_fusion
  255.4 1.7 reshape.403
  257.2 0.7 slice_reduce_fusion
  258.0 0.9 slice.117
  259.7 1.3 fusion.182
  261.4 9.4 %all-reduce.1 = (f32[32,64]{1,0:T(8,128)S(1)}, f32[64]{0:T(128)S(1)}) all-reduce(f32[32,64]{1,0:T(8,128)S(1)} %fusion.53, f32[64]{0:T(128)S(1)} %get-tuple-element.44), channel_id=1, replica_groups=mesh['seq'=64,'chan'=2] {'chan'}, use_global_device_ids=true, to_apply=%region_0.1 | all-reduce | flops 2112 | bytes 16896 | tf_op jit(solution)/shard_map/psum | solution.py:13
  270.8 270.4 %all-reduce = (f32[32,64]{1,0:T(8,128)S(1)}, f32[64]{0:T(128)S(1)}, f32[64,64]{1,0:T(8,128)S(1)}) all-reduce(f32[32,64]{1,0:T(8,128)S(1)} %get-tuple-element.10, f32[64]{0:T(128)S(1)} %get-tuple-element.11, f32[64,64]{1,0:T(8,128)S(1)} %fusion.40), channel_id=1, replica_groups=mesh['seq'=64,'chan'=2] {'seq'}, use_global_device_ids=true, to_apply=%region_1.2 | all-reduce | flops 6208 | bytes 49664 | tf_op jit(solution)/shard_map/psum | solution.py:13
  541.8 10.6 %all-to-all-start.3 = ((bf16[64,2,1024]{2,1,0:T(2,128)(2,1)}), bf16[64,2,1024]{2,1,0:T(2,128)(2,1)S(1)}, u32[]{:S(2)}, u32[]{:S(2)}) async-start(bf16[64,2,1024]{2,1,0:T(2,128)(2,1)} %slice.117), calls=%async_computation.3 | async-start | bytes 524288 | tf_op jit(solution)/shard_map/all_to_all | solution.py:150
  553.5 8.6 %all-to-all-done.3 = bf16[64,2,1024]{2,1,0:T(2,128)(2,1)S(1)} async-done(((bf16[64,2,1024]{2,1,0:T(2,128)(2,1)}), bf16[64,2,1024]{2,1,0:T(2,128)(2,1)S(1)}, u32[]{:S(2)}, u32[]{:S(2)}) %all-to-all-start.3) | async-done | bytes 262176 | tf_op jit(solution)/shard_map/all_to_all | solution.py:150
  562.1 1.1 slice_reduce_fusion.1
  563.2 0.7 reshape_squeeze.10
  563.9 0.7 reshape_squeeze.9
  (61 shorter events, 7.8 us)
Async XLA Ops:
  0.6 19.2 %copy-start = (f32[64,64]{1,0:T(8,128)S(1)}, f32[64,64]{1,0:T(8,128)}, u32[]{:S(2)}) copy-start(f32[64,64]{1,0:T(8,128)} %param.12) | copy-start | bytes 49156
  4.4 20.4 %all-to-all-start = ((bf16[64,2,1024]{2,1,0:T(2,128)(2,1)}), bf16[64,2,1024]{2,1,0:T(2,128)(2,1)S(1)}, u32[]{:S(2)}, u32[]{:S(2)}) async-start(bf16[64,2,1024]{2,1,0:T(2,128)(2,1)} %pad_maximum_fusion.14), calls=%async_computation | async-start | bytes 524288 | tf_op jit(solution)/shard_map/all_to_all | solution.py:70
  17.2 2.7 copy-start.13
  34.0 47.4 %all-to-all-start.1 = ((f32[128,2,3,1024]{3,1,2,0:T(2,128)}), f32[128,2,3,1024]{3,1,2,0:T(2,128)S(1)}, u32[]{:S(2)}, u32[]{:S(2)}) async-start(f32[128,2,3,1024]{3,1,2,0:T(2,128)} %copy.76), calls=%async_computation.1 | async-start | bytes 6291456 | tf_op jit(solution)/shard_map/all_to_all | solution.py:87
  42.2 0.6 copy-start.15
  111.4 5.5 copy-start.1
  111.4 5.5 copy-start.2
  111.4 5.5 copy-start.3
  127.6 6.8 %copy-start.6 = (f32[64,2,1,16,64]{4,3,2,1,0:T(8,128)}, f32[64,2,1,16,64]{4,3,2,1,0:T(8,128)S(1)}, u32[]{:S(2)}) copy-start(f32[64,2,1,16,64]{4,3,2,1,0:T(8,128)S(1)} %get-tuple-element.16) | copy-start | bytes 1572868
  128.3 6.0 %copy-start.4 = (f32[64,2,1,16,64]{4,3,2,1,0:T(8,128)}, f32[64,2,1,16,64]{4,3,2,1,0:T(8,128)S(1)}, u32[]{:S(2)}) copy-start(f32[64,2,1,16,64]{4,3,2,1,0:T(8,128)S(1)} %get-tuple-element.12) | copy-start | bytes 1572868
  128.3 6.0 %copy-start.5 = (f32[64,2,1,16,64]{4,3,2,1,0:T(8,128)}, f32[64,2,1,16,64]{4,3,2,1,0:T(8,128)S(1)}, u32[]{:S(2)}) copy-start(f32[64,2,1,16,64]{4,3,2,1,0:T(8,128)S(1)} %get-tuple-element.13) | copy-start | bytes 1572868
  150.3 4.6 copy-start.7
  150.3 4.6 copy-start.10
  150.3 4.6 copy-start.11
  173.3 7.0 %copy-start.8 = (f32[64,2,1024]{2,1,0:T(2,128)S(1)}, f32[64,2,1024]{2,1,0:T(2,128)}, u32[]{:S(2)}) copy-start(f32[64,2,1024]{2,1,0:T(2,128)} %get-tuple-element.28) | copy-start | bytes 1572868
  173.3 7.0 %copy-start.9 = (f32[64,2,1024]{2,1,0:T(2,128)S(1)}, f32[64,2,1024]{2,1,0:T(2,128)}, u32[]{:S(2)}) copy-start(f32[64,2,1024]{2,1,0:T(2,128)} %get-tuple-element.29) | copy-start | bytes 1572868
  188.9 46.3 %all-to-all-start.2 = ((f32[64,2,2,3,1024]{4,2,3,1,0:T(2,128)}), f32[64,2,2,3,1024]{4,2,3,1,0:T(2,128)S(1)}, u32[]{:S(2)}, u32[]{:S(2)}) async-start(f32[64,2,2,3,1024]{4,2,3,1,0:T(2,128)} %copy.86), calls=%async_computation.2 | async-start | bytes 6291456 | tf_op jit(solution)/shard_map/all_to_all | solution.py:145
  255.4 4.2 copy-start.12
  255.4 5.6 copy-start.14
  541.8 20.3 %all-to-all-start.3 = ((bf16[64,2,1024]{2,1,0:T(2,128)(2,1)}), bf16[64,2,1024]{2,1,0:T(2,128)(2,1)S(1)}, u32[]{:S(2)}, u32[]{:S(2)}) async-start(bf16[64,2,1024]{2,1,0:T(2,128)(2,1)} %slice.117), calls=%async_computation.3 | async-start | bytes 524288 | tf_op jit(solution)/shard_map/all_to_all | solution.py:150
